TPU v7x, 256 devices: a whole 4x4x8 slice. The times are simulated.
256 devices in a mesh: space: 32 (over z_hi, x, core), scen: 8 (over y, z_lo).
Axes of the slice: x: 4, y: 4, z: 8 (z_hi: 4, z_lo: 2; z = z_hi * 2 + z_lo), core: 2. Of those that a mesh axis runs over, the one named last changes fastest.
Arguments:
- concentration: float32 [8, 8, 6, 384, 384], P('scen', None, None, 'space'), may hold values from -6 to 6
- emissions: float32 [8, 6, 384, 384], P('scen', None, 'space'), may hold values from -3 to 3
- courant: float32 [2, 8, 6, 384, 384], P(None, None, None, 'space'), may hold values from -0.9 to 0.9
- tile_source: int32 [8640], P('space'), may hold values from 0 to 215, as said below
- tile_target: int32 [8640], P('space'), may hold values from 0 to 1023, as said below
- intersection: bfloat16 [8640, 128, 128], P('space'), may hold values from 0 to 0.0625
Outputs:
- transported: float32 [8, 8, 6, 384, 384], P('scen', None, None, 'space')
- regridded: float32 [8, 8, 1024, 128], P('scen', None, 'space')
- ensemble_moments: float32 [2, 8, 1024, 128], P(None, None, 'space')
Inputs may be any that keep to these rules, and one draw needn't show every extreme that they name: `tile_source`: every source block of a row band is named by at least one of the band's tiles. `tile_target`: latitude band b holds target blocks b * 32 to (b+1) * 32 - 1. The 270 tiles of one row band name at most 16 blocks of any one latitude band and at least 8 of every latitude band but one, which receives exactly 16 tiles from every row band. Every target block is named by some tile.
All inputs are finite; a program needn't handle non-finite values.
Results may differ from a plain program's by a relative error of at most 0.0027.
Values sent between devices are 32-bit elements; how exact they have to be, the bound alone decides.
No kernel may reach another device: no remote copies, remote signals or barrier semaphores. Data moves between devices by JAX's collectives and lax.ppermute only.
A program may use at most 128 MiB of HBM per device.

v0:
```python
import jax
import jax.numpy as jnp
from jax import lax
from jax.sharding import PartitionSpec as P

TGT_DEV = 32
SLOTS = 16


def from_behind(block, axis, distance):
    devices = range(lax.axis_size(axis))
    route = [((i - distance) % len(devices), i) for i in devices]
    return lax.ppermute(block, axis, route)


def parabola_sweep(padded, courant_faces, sweep_axis):
    cells_along = padded.shape[sweep_axis] - 6

    def window(values_in, first_cell, length):
        return lax.slice_in_dim(values_in, first_cell, first_cell + length, axis=sweep_axis)

    edge_values = 7.0 / 12.0 * (
        window(padded, 1, cells_along + 3) + window(padded, 2, cells_along + 3)
    ) - 1.0 / 12.0 * (window(padded, 0, cells_along + 3) + window(padded, 3, cells_along + 3))
    left_edge = window(edge_values, 0, cells_along + 2)
    right_edge = window(edge_values, 1, cells_along + 2)
    centre = window(padded, 2, cells_along + 2)
    slopes = right_edge - left_edge
    curvature = 6.0 * centre - 3.0 * (left_edge + right_edge)
    backward = -courant_faces
    upwind_left = courant_faces * (
        window(right_edge, 0, cells_along + 1)
        - 0.5
        * courant_faces
        * (
            window(slopes, 0, cells_along + 1)
            - (1.0 - 2.0 * courant_faces / 3.0) * window(curvature, 0, cells_along + 1)
        )
    )
    upwind_right = courant_faces * (
        window(left_edge, 1, cells_along + 1)
        + 0.5
        * backward
        * (
            window(slopes, 1, cells_along + 1)
            + (1.0 - 2.0 * backward / 3.0) * window(curvature, 1, cells_along + 1)
        )
    )
    fluxes = jnp.where(courant_faces >= 0.0, upwind_left, upwind_right)
    return window(padded, 3, cells_along) - (
        window(fluxes, 1, cells_along) - window(fluxes, 0, cells_along)
    )


def by_destination(values, band_count):
    width = values.shape[-1]
    blocks = values.reshape(values.shape[:-1] + (band_count, width // band_count))
    return jnp.flip(jnp.moveaxis(blocks, -2, 0), 0).reshape(band_count, -1)


def pack_rows(tracer, north_wind, lowest):
    row_count = tracer.shape[3]
    width_cells = tracer.shape[4]
    if lowest:
        layers = tracer[:, :, :, 0:3, :]
    else:
        layers = tracer[:, :, :, row_count - 3 :, :]
    parts = [layers.reshape(-1, width_cells)]
    if north_wind is not None:
        wind_row = north_wind[:, :, 0:1, :] if lowest else north_wind[:, :, row_count - 1 :, :]
        parts.append(wind_row.reshape(-1, width_cells))
    return jnp.concatenate(parts, 0)


def edge_rows(tracer, north_wind, position, band_count, with_wind):
    row_count = tracer.shape[3]
    top_parts = [by_destination(tracer[:, :, 0::2, row_count - 3 :, :], band_count)]
    low_parts = [by_destination(tracer[:, :, 1::2, 0:3, :], band_count)]
    if with_wind:
        top_parts.append(by_destination(north_wind[:, 0::2, row_count - 1, :], band_count))
        low_parts.append(by_destination(north_wind[:, 1::2, 0, :], band_count))
    send_top = jnp.concatenate(top_parts, 1)
    send_low = jnp.concatenate(low_parts, 1)
    send = jnp.where(
        position == band_count - 1, send_top, jnp.where(position == 0, send_low, 0.0)
    ).astype(send_top.dtype)
    got = lax.all_to_all(send, "space", 0, 0, tiled=True)
    return (got[band_count - 1], got[0])


def column_halos(tracer, east_wind, north_wind, position, band_count, edge_wind):
    scenarios, levels, _, row_count, width_cells = tracer.shape
    top, low = edge_rows(tracer, north_wind, position, band_count, edge_wind is None)
    cells = scenarios * levels * 3 * 3 * row_count
    top_layers = top[:cells].reshape(scenarios, levels, 3, 3, row_count)
    low_layers = low[:cells].reshape(scenarios, levels, 3, 3, row_count)
    if edge_wind is None:
        edge_wind = (
            top[cells:].reshape(levels, 3, row_count),
            low[cells:].reshape(levels, 3, row_count),
        )
    top_wind, low_wind = edge_wind
    padded_faces = []
    speed_faces = []
    for face_number in range(6):
        half = face_number // 2
        if face_number % 2 == 0:
            source = top_layers[:, :, (half - 1) % 3]
            west_cells = jnp.swapaxes(jnp.flip(source, -1), -1, -2)
            west_speed = jnp.flip(top_wind[:, (half - 1) % 3], -1)
            east_cells = tracer[:, :, (face_number + 1) % 6, :, 0:3]
            east_speed = east_wind[:, (face_number + 1) % 6, :, 0]
        else:
            west_cells = tracer[:, :, (face_number - 1) % 6, :, width_cells - 3 :]
            west_speed = east_wind[:, (face_number - 1) % 6, :, width_cells - 1]
            source = low_layers[:, :, (half + 1) % 3]
            east_cells = jnp.swapaxes(jnp.flip(source, -1), -1, -2)
            east_speed = jnp.flip(low_wind[:, (half + 1) % 3], -1)
        padded_faces.append(
            jnp.concatenate([west_cells, tracer[:, :, face_number], east_cells], -1)
        )
        speeds = jnp.concatenate(
            [west_speed[:, :, None], east_wind[:, face_number], east_speed[:, :, None]], -1
        )
        speed_faces.append(0.5 * (speeds[:, :, :-1] + speeds[:, :, 1:]))
    return (jnp.stack(padded_faces, 2), jnp.stack(speed_faces, 1), edge_wind)


def edge_columns(tracer, east_wind, position, band_count, with_wind):
    scenarios, levels, _, row_count, width_cells = tracer.shape
    to_top = [jnp.swapaxes(tracer[:, :, 0::2, :, 0:3], -1, -2).reshape(-1)]
    to_low = [jnp.swapaxes(tracer[:, :, 1::2, :, width_cells - 3 :], -1, -2).reshape(-1)]
    if with_wind:
        to_top.append(east_wind[:, 0::2, :, 0].reshape(-1))
        to_low.append(east_wind[:, 1::2, :, width_cells - 1].reshape(-1))
    to_top = jnp.concatenate(to_top)
    to_low = jnp.concatenate(to_low)
    send = jnp.zeros((band_count,) + to_top.shape, to_top.dtype)
    send = send.at[band_count - 1].set(to_top).at[0].set(to_low)
    got = lax.all_to_all(send, "space", 0, 0, tiled=True)
    cells = scenarios * levels * 3 * 3 * row_count
    layers = got[:, :cells].reshape(band_count, scenarios, levels, 3, 3, row_count)
    layers = jnp.moveaxis(layers, 0, -2).reshape(scenarios, levels, 3, 3, band_count * row_count)
    wind = None
    if with_wind:
        wind = got[:, cells:].reshape(band_count, levels, 3, row_count)
        wind = jnp.moveaxis(wind, 0, -2).reshape(levels, 3, band_count * row_count)
    return (layers, wind)


def row_halos(tracer, east_wind, north_wind, position, band_count, row_wind):
    first_step = row_wind is None
    shifted = []
    for step_by, lowest in ((-1, True), (1, False)):
        packed = pack_rows(tracer, north_wind if first_step else None, lowest)
        shifted.append(from_behind(packed, "space", step_by))
    edge_layers, edge_speed = edge_columns(tracer, east_wind, position, band_count, first_step)
    layer_rows = tracer.shape[0] * tracer.shape[1] * 18
    width_cells = tracer.shape[4]
    if first_step:
        levels = tracer.shape[1]
        row_wind = tuple(
            (packed[layer_rows:].reshape(levels, 6, width_cells) for packed in shifted)
        ) + (edge_speed,)
    above_wind, below_wind, edge_speed = row_wind
    above_layers, below_layers = (
        packed[:layer_rows].reshape(tracer.shape[0], tracer.shape[1], 6, 3, width_cells)
        for packed in shifted
    )
    at_top = position == band_count - 1
    at_bottom = position == 0
    padded_faces = []
    speed_faces = []
    for face_number in range(6):
        half = face_number // 2
        if face_number % 2 == 0:
            north_cells = jnp.where(
                at_top,
                jnp.flip(edge_layers[:, :, (half + 1) % 3], -1),
                above_layers[:, :, face_number],
            )
            north_speed = jnp.where(
                at_top, jnp.flip(edge_speed[:, (half + 1) % 3], -1), above_wind[:, face_number]
            )
            south_cells = jnp.where(
                at_bottom,
                below_layers[:, :, (face_number - 1) % 6],
                below_layers[:, :, face_number],
            )
            south_speed = jnp.where(
                at_bottom, below_wind[:, (face_number - 1) % 6], below_wind[:, face_number]
            )
        else:
            north_cells = jnp.where(
                at_top, above_layers[:, :, (face_number + 1) % 6], above_layers[:, :, face_number]
            )
            north_speed = jnp.where(
                at_top, above_wind[:, (face_number + 1) % 6], above_wind[:, face_number]
            )
            south_cells = jnp.where(
                at_bottom,
                jnp.flip(edge_layers[:, :, (half - 1) % 3], -1),
                below_layers[:, :, face_number],
            )
            south_speed = jnp.where(
                at_bottom, jnp.flip(edge_speed[:, (half - 1) % 3], -1), below_wind[:, face_number]
            )
        padded_faces.append(
            jnp.concatenate([south_cells, tracer[:, :, face_number], north_cells], -2)
        )
        speeds = jnp.concatenate(
            [south_speed[:, None, :], north_wind[:, face_number], north_speed[:, None, :]], -2
        )
        speed_faces.append(0.5 * (speeds[:, :-1, :] + speeds[:, 1:, :]))
    return (jnp.stack(padded_faces, 2), jnp.stack(speed_faces, 1), row_wind)


def regrid(tracer, tile_source, tile_target, intersection, band_count):
    scenarios = tracer.shape[0]
    levels = tracer.shape[1]
    batch_rows = scenarios * levels
    block_cells = intersection.shape[1]
    blocks = tracer.astype(jnp.bfloat16).reshape(batch_rows, -1, block_cells)
    chosen = jnp.take(blocks, tile_source, axis=1)
    partial_value = jnp.einsum(
        "btk,tkc->tbc", chosen, intersection, preferred_element_type=jnp.float32
    )
    target_band = tile_target // TGT_DEV
    target_block = tile_target % TGT_DEV
    band_hot = (target_band[:, None] == jnp.arange(band_count)[None, :]).astype(jnp.int32)
    rank = jnp.sum((jnp.cumsum(band_hot, 0) - band_hot) * band_hot, 1)
    slot = jnp.where(rank < SLOTS, target_band * SLOTS + rank, -1)
    slot_hot = (slot[None, :] == jnp.arange(band_count * SLOTS)[:, None]).astype(jnp.float32)
    slotted = jnp.einsum("st,tbc->sbc", slot_hot, partial_value, precision=lax.Precision.HIGHEST)
    slot_block = jnp.sum(slot_hot * target_block[None, :].astype(jnp.float32), 1)
    index_rows = jnp.zeros((band_count, 8, block_cells), jnp.float32)
    index_rows = index_rows.at[:, 0, :SLOTS].set(slot_block.reshape(band_count, SLOTS))
    send = jnp.concatenate(
        [slotted.reshape(band_count, SLOTS * batch_rows, block_cells), index_rows], 1
    )
    got = lax.all_to_all(send, "space", 0, 0, tiled=True)
    values = got[:, : SLOTS * batch_rows].reshape(band_count * SLOTS, batch_rows, block_cells)
    got_block = got[:, SLOTS * batch_rows, :SLOTS].reshape(-1)
    block_hot = (got_block[None, :] == jnp.arange(TGT_DEV)[:, None].astype(jnp.float32)).astype(
        jnp.float32
    )
    summed = jnp.einsum("ks,sbc->bkc", block_hot, values, precision=lax.Precision.HIGHEST)
    return summed.reshape(scenarios, levels, TGT_DEV, block_cells)


def local(concentration, emissions, courant, tile_source, tile_target, intersection):
    band_count = lax.axis_size("space")
    position = lax.axis_index("space")
    tracer = concentration.at[:, 0].add(emissions)
    east_wind = courant[0]
    north_wind = courant[1]
    edge_wind = None
    row_wind = None
    for step_number in range(2):
        padded, courant_faces, edge_wind = column_halos(
            tracer, east_wind, north_wind, position, band_count, edge_wind
        )
        tracer = parabola_sweep(padded, courant_faces, 4)
        padded, courant_faces, row_wind = row_halos(
            tracer, east_wind, north_wind, position, band_count, row_wind
        )
        tracer = parabola_sweep(padded, courant_faces, 3)
    regridded = regrid(tracer, tile_source, tile_target, intersection, band_count)
    scenarios = tracer.shape[0]
    everyone = lax.all_gather(regridded, "scen", axis=0, tiled=True)
    moment_sums = jnp.stack([jnp.sum(everyone, 0), jnp.sum(everyone * everyone, 0)])
    ensemble_moments = moment_sums / (scenarios * lax.axis_size("scen"))
    return (tracer, regridded, ensemble_moments)


def solution(mesh):
    return jax.shard_map(
        local,
        mesh=mesh,
        in_specs=(
            P("scen", None, None, "space", None),
            P("scen", None, "space", None),
            P(None, None, None, "space", None),
            P("space"),
            P("space"),
            P("space", None, None),
        ),
        out_specs=(
            P("scen", None, None, "space", None),
            P("scen", None, "space", None),
            P(None, None, "space", None),
        ),
        check_vma=False,
    )
```

profile of v0, /device:TPU:2, one launch (start us, length us, event | category | flops | bytes accessed | tf_op | source)
XLA Modules:
  0.0 335.2 jit_solution(12581908648371963601)
XLA Ops:
  23.3 12.0 %all-to-all-start = ((f32[32,1,1152]{2,1,0:T(1,128)}), f32[32,1,1152]{2,1,0:T(1,128)S(1)}, u32[]{:S(2)}, u32[]{:S(2)}) async-start(f32[32,1,1152]{2,1,0:T(1,128)} %copy.508), calls=%async_computation | async-start | bytes 294912 | tf_op jit(solution)/shard_map/all_to_all | solution.py:87
  71.1 1.8 copy.527
  73.9 1.8 copy.525
  80.4 9.8 %all-to-all-start.1 = ((f32[32,1,1152]{2,1,0:T(1,128)}), f32[32,1,1152]{2,1,0:T(1,128)}, u32[]{:S(2)}, u32[]{:S(2)}) async-start(f32[32,1,1152]{2,1,0:T(1,128)} %copy.530), calls=%async_computation.1 | async-start | bytes 294912 | tf_op jit(solution)/shard_map/all_to_all | solution.py:140
  92.0 1.8 reshape.3064
  107.1 2.1 reshape.3108
  114.0 2.2 rev.143
  132.8 3.2 reshape.3080
  136.0 3.0 rev.149
  139.1 3.2 reshape.3079
  142.3 3.0 rev.148
  146.6 2.3 copy.573
  148.9 1.8 copy.574
  150.7 14.9 %all-to-all-start.2 = ((f32[32,1,864]{2,1,0:T(1,128)}), f32[32,1,864]{2,1,0:T(1,128)}, u32[]{:S(2)}, u32[]{:S(2)}) async-start(f32[32,1,864]{2,1,0:T(1,128)} %copy.574), calls=%async_computation.2 | async-start | bytes 229376 | tf_op jit(solution)/shard_map/all_to_all | solution.py:87
  166.4 8.3 %all-to-all-done.2 = f32[32,1,864]{2,1,0:T(1,128)} async-done(((f32[32,1,864]{2,1,0:T(1,128)}), f32[32,1,864]{2,1,0:T(1,128)}, u32[]{:S(2)}, u32[]{:S(2)}) %all-to-all-start.2) | async-done | bytes 110624 | tf_op jit(solution)/shard_map/all_to_all | solution.py:87
  186.2 5.2 %all-to-all-start.3 = ((f32[32,1,864]{2,1,0:T(1,128)}), f32[32,1,864]{2,1,0:T(1,128)S(1)}, u32[]{:S(2)}, u32[]{:S(2)}) async-start(f32[32,1,864]{2,1,0:T(1,128)} %copy.587), calls=%async_computation.3 | async-start | bytes 229376 | tf_op jit(solution)/shard_map/all_to_all | solution.py:140
  192.0 1.9 collective-permute-start.3
  193.9 7.1 %all-to-all-done.3 = f32[32,1,864]{2,1,0:T(1,128)S(1)} async-done(((f32[32,1,864]{2,1,0:T(1,128)}), f32[32,1,864]{2,1,0:T(1,128)S(1)}, u32[]{:S(2)}, u32[]{:S(2)}) %all-to-all-start.3) | async-done | bytes 110624 | tf_op jit(solution)/shard_map/all_to_all | solution.py:140
  208.3 1.8 gather_fusion
  210.1 4.9 %fusion.62 = f32[270,8,128]{2,1,0:T(8,128)S(1)} fusion(bf16[270,128,128]{2,1,0:T(8,128)(2,1)} %param.23, bf16[270,8,128]{2,1,0:T(8,128)(2,1)S(1)} %gather_fusion, pred[270]{0:T(512)(128)(4,1)S(1)} %copy-done.61), kind=kOutput, calls=%fused_computation.103 | convolution fusion | flops 71055360 | bytes 10506510 | tf_op jit(solution)/shard_map/btk,tkc->tbc/dot_general | solution.py:225
  215.0 2.0 fusion.28
  219.8 9.5 %all-to-all-start.4 = ((f32[32,136,128]{2,1,0:T(8,128)}), f32[32,136,128]{2,1,0:T(8,128)S(1)}, u32[]{:S(2)}, u32[]{:S(2)}) async-start(f32[32,136,128]{2,1,0:T(8,128)} %select_maximum_fusion), calls=%async_computation.4 | async-start | bytes 4456448 | tf_op jit(solution)/shard_map/all_to_all | solution.py:241
  229.4 52.0 %all-to-all-done.4 = f32[32,136,128]{2,1,0:T(8,128)S(1)} async-done(((f32[32,136,128]{2,1,0:T(8,128)}), f32[32,136,128]{2,1,0:T(8,128)S(1)}, u32[]{:S(2)}, u32[]{:S(2)}) %all-to-all-start.4) | async-done | bytes 2228256 | tf_op jit(solution)/shard_map/all_to_all | solution.py:241
  283.5 42.5 %all-gather.3.cloned.1.call-done = f32[64,32,128]{2,1,0:T(8,128)} async-done(((f32[8,32,128]{2,1,0:T(8,128)}), f32[64,32,128]{2,1,0:T(8,128)}) %all-gather.3.cloned.1.call-update) | async-done | bytes 1048592 | tf_op jit(solution)/shard_map/all_gather | solution.py:270
  (424 shorter events, 120.7 us)
Async XLA Ops:
  21.1 14.2 %copy-start.60 = (s32[270]{0:T(512)S(1)}, s32[270]{0:T(512)}, u32[]{:S(2)}) copy-start(s32[270]{0:T(512)} %param.21) | copy-start | bytes 3244
  23.3 22.2 %all-to-all-start = ((f32[32,1,1152]{2,1,0:T(1,128)}), f32[32,1,1152]{2,1,0:T(1,128)S(1)}, u32[]{:S(2)}, u32[]{:S(2)}) async-start(f32[32,1,1152]{2,1,0:T(1,128)} %copy.508), calls=%async_computation | async-start | bytes 294912 | tf_op jit(solution)/shard_map/all_to_all | solution.py:87
  58.4 5.9 %copy-start.16 = (f32[1,8,12,384]{3,1,2,0:T(8,128)S(1)}, f32[1,8,12,384]{3,1,2,0:T(8,128)}, u32[]{:S(2)}) copy-start(f32[1,8,12,384]{3,1,2,0:T(8,128)} %get-tuple-element.157) | copy-start | bytes 442372
  69.5 4.3 %copy-start.59 = (f32[288]{0:T(512)S(1)}, f32[288]{0:T(512)}, u32[]{:S(2)}) copy-start(f32[288]{0:T(512)} %reshape_squeeze.21) | copy-start | bytes 3460
  69.5 7.0 %copy-start.58 = (f32[288]{0:T(512)S(1)}, f32[288]{0:T(512)}, u32[]{:S(2)}) copy-start(f32[288]{0:T(512)} %reshape_squeeze.20) | copy-start | bytes 3460
  80.4 22.2 %all-to-all-start.1 = ((f32[32,1,1152]{2,1,0:T(1,128)}), f32[32,1,1152]{2,1,0:T(1,128)}, u32[]{:S(2)}, u32[]{:S(2)}) async-start(f32[32,1,1152]{2,1,0:T(1,128)} %copy.530), calls=%async_computation.1 | async-start | bytes 294912 | tf_op jit(solution)/shard_map/all_to_all | solution.py:140
  99.0 18.6 %collective-permute-start.1 = (f32[192,384]{1,0:T(8,128)}, f32[192,384]{1,0:T(8,128)}, u32[]{:S(2)}, u32[]{:S(2)}) collective-permute-start(f32[192,384]{1,0:T(8,128)} %pad_maximum_fusion.1), channel_id=1, source_target_pairs={{8,0},{16,8},{24,16},{32,24},{40,32},{48,40},{56,48},{64,56},{72,6... | collective-permute-start | bytes 884744 | tf_op jit(solution)/shard_map/ppermute | solution.py:13
  100.8 18.4 %collective-permute-start = (f32[192,384]{1,0:T(8,128)}, f32[192,384]{1,0:T(8,128)}, u32[]{:S(2)}, u32[]{:S(2)}) collective-permute-start(f32[192,384]{1,0:T(8,128)} %pad_maximum_fusion), channel_id=1, source_target_pairs={{248,0},{0,8},{8,16},{16,24},{24,32},{32,40},{40,48},{48,56},{56,6... | collective-permute-start | bytes 884744 | tf_op jit(solution)/shard_map/ppermute | solution.py:13
  110.1 6.1 %copy-start.41 = (f32[1,8,3,384]{3,2,1,0:T(4,128)S(1)}, f32[1,8,3,384]{3,2,1,0:T(4,128)}, u32[]{:S(2)}) copy-start(f32[1,8,3,384]{3,2,1,0:T(4,128)} %get-tuple-element.196) | copy-start | bytes 110596
  110.1 11.3 %copy-start.9 = (f32[8,1,12,384]{3,0,2,1:T(8,128)S(1)}, f32[8,1,12,384]{3,0,2,1:T(8,128)}, u32[]{:S(2)}) copy-start(f32[8,1,12,384]{3,0,2,1:T(8,128)} %get-tuple-element.124) | copy-start | bytes 442372
  150.7 24.0 %all-to-all-start.2 = ((f32[32,1,864]{2,1,0:T(1,128)}), f32[32,1,864]{2,1,0:T(1,128)}, u32[]{:S(2)}, u32[]{:S(2)}) async-start(f32[32,1,864]{2,1,0:T(1,128)} %copy.574), calls=%async_computation.2 | async-start | bytes 229376 | tf_op jit(solution)/shard_map/all_to_all | solution.py:87
  166.4 13.1 %copy-start.21 = (f32[1,8,12,384]{3,1,2,0:T(8,128)S(1)}, f32[1,8,12,384]{3,1,2,0:T(8,128)}, u32[]{:S(2)}) copy-start(f32[1,8,12,384]{3,1,2,0:T(8,128)} %get-tuple-element.115) | copy-start | bytes 442372
  166.4 13.1 %copy-start.40 = (f32[1,8,12,3]{3,1,2,0:T(8,128)S(1)}, f32[1,8,12,3]{3,1,2,0:T(8,128)}, u32[]{:S(2)}) copy-start(f32[1,8,12,3]{3,1,2,0:T(8,128)} %get-tuple-element.109) | copy-start | bytes 3460
  166.4 13.3 %copy-start.20 = (f32[1,8,12,384]{3,1,2,0:T(8,128)S(1)}, f32[1,8,12,384]{3,1,2,0:T(8,128)}, u32[]{:S(2)}) copy-start(f32[1,8,12,384]{3,1,2,0:T(8,128)} %get-tuple-element.114) | copy-start | bytes 442372
  166.4 13.3 %copy-start.39 = (f32[1,8,12,3]{3,1,2,0:T(8,128)S(1)}, f32[1,8,12,3]{3,1,2,0:T(8,128)}, u32[]{:S(2)}) copy-start(f32[1,8,12,3]{3,1,2,0:T(8,128)} %get-tuple-element.108) | copy-start | bytes 3460
  166.4 14.2 %copy-start.19 = (f32[1,8,12,384]{3,1,2,0:T(8,128)S(1)}, f32[1,8,12,384]{3,1,2,0:T(8,128)}, u32[]{:S(2)}) copy-start(f32[1,8,12,384]{3,1,2,0:T(8,128)} %get-tuple-element.113) | copy-start | bytes 442372
  166.4 14.2 %copy-start.38 = (f32[1,8,12,3]{3,1,2,0:T(8,128)S(1)}, f32[1,8,12,3]{3,1,2,0:T(8,128)}, u32[]{:S(2)}) copy-start(f32[1,8,12,3]{3,1,2,0:T(8,128)} %get-tuple-element.107) | copy-start | bytes 3460
  176.0 4.7 %copy-start.37 = (f32[1,8,12,3]{3,1,2,0:T(8,128)S(1)}, f32[1,8,12,3]{3,1,2,0:T(8,128)}, u32[]{:S(2)}) copy-start(f32[1,8,12,3]{3,1,2,0:T(8,128)} %get-tuple-element.106) | copy-start | bytes 3460
  186.2 14.8 %all-to-all-start.3 = ((f32[32,1,864]{2,1,0:T(1,128)}), f32[32,1,864]{2,1,0:T(1,128)S(1)}, u32[]{:S(2)}, u32[]{:S(2)}) async-start(f32[32,1,864]{2,1,0:T(1,128)} %copy.587), calls=%async_computation.3 | async-start | bytes 229376 | tf_op jit(solution)/shard_map/all_to_all | solution.py:140
  191.6 12.7 %collective-permute-start.2 = (f32[144,384]{1,0:T(8,128)S(1)}, f32[144,384]{1,0:T(8,128)S(1)}, u32[]{:S(2)}, u32[]{:S(2)}) collective-permute-start(f32[144,384]{1,0:T(8,128)S(1)} %reshape.3081), channel_id=1, source_target_pairs={{248,0},{0,8},{8,16},{16,24},{24,32},{32,40},{40,48},{48,56},{56,6... | collective-permute-start | bytes 663560 | tf_op jit(solution)/shard_map/ppermute | solution.py:13
  192.0 12.5 %collective-permute-start.3 = (f32[144,384]{1,0:T(8,128)S(1)}, f32[144,384]{1,0:T(8,128)S(1)}, u32[]{:S(2)}, u32[]{:S(2)}) collective-permute-start(f32[144,384]{1,0:T(8,128)S(1)} %reshape.3086), channel_id=1, source_target_pairs={{8,0},{16,8},{24,16},{32,24},{40,32},{48,40},{56,48},{64,56},{72,6... | collective-permute-start | bytes 663560 | tf_op jit(solution)/shard_map/ppermute | solution.py:13
  210.1 4.9 %copy-start.56 = (s32[270]{0:T(512)S(1)}, s32[270]{0:T(512)}, u32[]{:S(2)}) copy-start(s32[270]{0:T(512)} %copy-done.55) | copy-start | bytes 3244
  219.8 61.6 %all-to-all-start.4 = ((f32[32,136,128]{2,1,0:T(8,128)}), f32[32,136,128]{2,1,0:T(8,128)S(1)}, u32[]{:S(2)}, u32[]{:S(2)}) async-start(f32[32,136,128]{2,1,0:T(8,128)} %select_maximum_fusion), calls=%async_computation.4 | async-start | bytes 4456448 | tf_op jit(solution)/shard_map/all_to_all | solution.py:241
  229.3 96.7 %all-gather.3.cloned.1.call-start = ((), (), s32[]{:S(2)}) async-start(), calls=%async_computation.5 | async-start | bytes 1179648 | tf_op jit(solution)/shard_map/all_gather | solution.py:270
  (49 other events, 78.4 us)
Sparse Core Ops, SparseCore 0:
  283.6 42.3 all-gather.2
where the time goes:
time: 341 us; the launch traced here: 335 us
  local copies, waits for them, and re-layouts  110 us (32%)
  waiting for transfers between devices  110 us (32%)
  starting transfers between devices  54.6 us (16%)
  other arithmetic  36.2 us (11%)
  between operations  16.2 us (5%)
  matrix products  8.66 us (3%)
    all_to_all x1, waiting for transfers between devices, regrid(): got = lax.all_to_all(send, 'space', 0, 0, tiled=True)  52 us
    all_gather x1, waiting for transfers between devices, local(): everyone = lax.all_gather(regridded, 'scen', axis=0, tiled=True)  42.5 us
    all_to_all x2, starting transfers between devices, edge_rows(): got = lax.all_to_all(send, 'space', 0, 0, tiled=True)  26.9 us
    all_to_all x2, starting transfers between devices, edge_columns(): got = lax.all_to_all(send, 'space', 0, 0, tiled=True)  15 us
    unnamed x40, other arithmetic  10.3 us
    all_to_all x1, starting transfers between devices, regrid(): got = lax.all_to_all(send, 'space', 0, 0, tiled=True)  9.5 us
    reshape x4, local copies, waits for them, and re-layouts, by_destination(): values.reshape(values.shape[:-1] + (band_count, width // band_count))  8.99 us
    rev x10, local copies, waits for them, and re-layouts, by_destination(): return jnp.flip(jnp.moveaxis(blocks, -2, 0), 0).reshape(band_count, -1)  8.87 us
  transfers between devices with their start and end apart: 10, of which 4 were waited for; matrix products, arithmetic and copies ran while one was open for 13% of the time, Pallas kernels for 0%

commit v1 on v0

--- a/solution.py
+++ b/solution.py
@@ -267,7 +267,9 @@
         tracer = parabola_sweep(padded, courant_faces, 3)
     regridded = regrid(tracer, tile_source, tile_target, intersection, band_count)
     scenarios = tracer.shape[0]
-    everyone = lax.all_gather(regridded, "scen", axis=0, tiled=True)
+    everyone = jnp.concatenate(
+        lax.all_to_all(jnp.stack([regridded] * lax.axis_size("scen")), "scen", 0, 0), axis=0
+    )
     moment_sums = jnp.stack([jnp.sum(everyone, 0), jnp.sum(everyone * everyone, 0)])
     ensemble_moments = moment_sums / (scenarios * lax.axis_size("scen"))
     return (tracer, regridded, ensemble_moments)

time: 341 us -> 306 us (0.90)
  the two profiles are of different devices: /device:TPU:2 before, /device:TPU:1 now
where the time goes in v1:
time: 306 us; the launch traced here: 300 us
  local copies, waits for them, and re-layouts  110 us (36%)
  waiting for transfers between devices  73.1 us (24%)
  starting transfers between devices  51.7 us (17%)
  other arithmetic  34.9 us (11%)
  blocking collectives  19.6 us (6%)
  matrix products  7.98 us (3%)
    all_to_all x1, waiting for transfers between devices, regrid(): got = lax.all_to_all(send, 'space', 0, 0, tiled=True)  53.8 us
    all_to_all x2, starting transfers between devices, edge_rows(): got = lax.all_to_all(send, 'space', 0, 0, tiled=True)  26.6 us
    all_to_all x1, blocking collectives, local(): lax.all_to_all(jnp.stack([regridded] * lax.axis_size('scen')), 'scen', 0, 0)  19.6 us
    all_to_all x2, starting transfers between devices, edge_columns(): got = lax.all_to_all(send, 'space', 0, 0, tiled=True)  12.5 us
    all_to_all x2, waiting for transfers between devices, edge_rows(): got = lax.all_to_all(send, 'space', 0, 0, tiled=True)  10.9 us
    unnamed x40, other arithmetic  10.4 us
    reshape x4, local copies, waits for them, and re-layouts, by_destination(): values.reshape(values.shape[:-1] + (band_count, width // band_count))  9.01 us
    rev x10, local copies, waits for them, and re-layouts, by_destination(): return jnp.flip(jnp.moveaxis(blocks, -2, 0), 0).reshape(band_count, -1)  8.9 us
  transfers between devices with their start and end apart: 9, of which 4 were waited for; matrix products, arithmetic and copies ran while one was open for 14% of the time, Pallas kernels for 0%

profile of v1, /device:TPU:1, one launch (start us, length us, event | category | flops | bytes accessed | tf_op | source)
XLA Modules:
  0.0 299.7 jit_solution(3051255712790396572)
XLA Ops:
  16.8 13.0 %all-to-all-start = ((f32[32,1,1152]{2,1,0:T(1,128)}), f32[32,1,1152]{2,1,0:T(1,128)S(1)}, u32[]{:S(2)}, u32[]{:S(2)}) async-start(f32[32,1,1152]{2,1,0:T(1,128)} %copy.508), calls=%async_computation | async-start | bytes 294912 | tf_op jit(solution)/shard_map/all_to_all | solution.py:87
  66.5 1.8 copy.527
  69.2 1.8 copy.525
  75.8 8.7 %all-to-all-start.1 = ((f32[32,1,1152]{2,1,0:T(1,128)}), f32[32,1,1152]{2,1,0:T(1,128)}, u32[]{:S(2)}, u32[]{:S(2)}) async-start(f32[32,1,1152]{2,1,0:T(1,128)} %copy.530), calls=%async_computation.1 | async-start | bytes 294912 | tf_op jit(solution)/shard_map/all_to_all | solution.py:140
  86.3 1.8 reshape.3068
  95.3 1.9 collective-permute-start
  102.6 2.1 reshape.3111
  109.5 2.2 rev.143
  128.3 3.2 %reshape.3084 = f32[1,8,3,3,32,12]{5,4,1,3,2,0:T(8,128)} reshape(f32[1,8,3,3,384]{4,1,3,2,0:T(8,128)} %get-tuple-element.117) | data formatting | bytes 221184 | tf_op jit(solution)/shard_map/reshape | solution.py:57
  131.5 3.1 %rev.149 = f32[32,1,8,3,3,12]{5,0,2,4,3,1:T(8,128)} reverse(f32[32,1,8,3,3,12]{5,0,2,4,3,1:T(8,128)} %bitcast.607), dimensions={0} | reverse | bytes 221184 | tf_op jit(solution)/shard_map/jit(_flip)/rev | solution.py:58
  134.6 3.2 %reshape.3083 = f32[1,8,3,3,32,12]{5,4,1,3,2,0:T(8,128)} reshape(f32[1,8,3,3,384]{4,1,3,2,0:T(8,128)} %get-tuple-element.118) | data formatting | bytes 221184 | tf_op jit(solution)/shard_map/reshape | solution.py:57
  137.8 3.1 %rev.148 = f32[32,1,8,3,3,12]{5,0,2,4,3,1:T(8,128)} reverse(f32[32,1,8,3,3,12]{5,0,2,4,3,1:T(8,128)} %bitcast.608), dimensions={0} | reverse | bytes 221184 | tf_op jit(solution)/shard_map/jit(_flip)/rev | solution.py:58
  142.2 2.3 copy.573
  144.5 1.8 copy.574
  146.3 13.6 %all-to-all-start.2 = ((f32[32,1,864]{2,1,0:T(1,128)}), f32[32,1,864]{2,1,0:T(1,128)}, u32[]{:S(2)}, u32[]{:S(2)}) async-start(f32[32,1,864]{2,1,0:T(1,128)} %copy.574), calls=%async_computation.2 | async-start | bytes 229376 | tf_op jit(solution)/shard_map/all_to_all | solution.py:87
  160.7 9.8 %all-to-all-done.2 = f32[32,1,864]{2,1,0:T(1,128)} async-done(((f32[32,1,864]{2,1,0:T(1,128)}), f32[32,1,864]{2,1,0:T(1,128)}, u32[]{:S(2)}, u32[]{:S(2)}) %all-to-all-start.2) | async-done | bytes 110624 | tf_op jit(solution)/shard_map/all_to_all | solution.py:87
  182.0 3.7 %all-to-all-start.3 = ((f32[32,1,864]{2,1,0:T(1,128)}), f32[32,1,864]{2,1,0:T(1,128)S(1)}, u32[]{:S(2)}, u32[]{:S(2)}) async-start(f32[32,1,864]{2,1,0:T(1,128)} %copy.587), calls=%async_computation.3 | async-start | bytes 229376 | tf_op jit(solution)/shard_map/all_to_all | solution.py:140
  188.2 8.4 %all-to-all-done.3 = f32[32,1,864]{2,1,0:T(1,128)S(1)} async-done(((f32[32,1,864]{2,1,0:T(1,128)}), f32[32,1,864]{2,1,0:T(1,128)S(1)}, u32[]{:S(2)}, u32[]{:S(2)}) %all-to-all-start.3) | async-done | bytes 110624 | tf_op jit(solution)/shard_map/all_to_all | solution.py:140
  203.8 1.8 gather_fusion
  205.6 4.9 %fusion.62 = f32[270,8,128]{2,1,0:T(8,128)S(1)} fusion(bf16[270,128,128]{2,1,0:T(8,128)(2,1)} %param.23, bf16[270,8,128]{2,1,0:T(8,128)(2,1)S(1)} %gather_fusion, pred[270]{0:T(512)(128)(4,1)S(1)} %copy-done.62), kind=kOutput, calls=%fused_computation.103 | convolution fusion | flops 71055360 | bytes 10506510 | tf_op jit(solution)/shard_map/btk,tkc->tbc/dot_general | solution.py:225
  210.6 2.0 fusion.28
  215.3 8.3 %all-to-all-start.4 = ((f32[32,136,128]{2,1,0:T(8,128)}), f32[32,136,128]{2,1,0:T(8,128)S(1)}, u32[]{:S(2)}, u32[]{:S(2)}) async-start(f32[32,136,128]{2,1,0:T(8,128)} %select_maximum_fusion), calls=%async_computation.4 | async-start | bytes 4456448 | tf_op jit(solution)/shard_map/all_to_all | solution.py:241
  223.7 53.8 %all-to-all-done.4 = f32[32,136,128]{2,1,0:T(8,128)S(1)} async-done(((f32[32,136,128]{2,1,0:T(8,128)}), f32[32,136,128]{2,1,0:T(8,128)S(1)}, u32[]{:S(2)}, u32[]{:S(2)}) %all-to-all-start.4) | async-done | bytes 2228256 | tf_op jit(solution)/shard_map/all_to_all | solution.py:241
  279.1 19.6 %all_to_all.53 = f32[8,1,8,32,128]{4,3,2,1,0:T(8,128)S(1)} all-to-all(f32[8,1,8,32,128]{4,3,2,1,0:T(8,128)S(1)} %stack.200), channel_id=1, replica_groups=mesh['space'=32,'scen'=8] {'scen'}, dimensions={0} | all-to-all | bytes 2097152 | tf_op jit(solution)/shard_map/all_to_all | solution.py:271
  (425 shorter events, 120.9 us)
Async XLA Ops:
  14.6 15.2 %copy-start.61 = (s32[270]{0:T(512)S(1)}, s32[270]{0:T(512)}, u32[]{:S(2)}) copy-start(s32[270]{0:T(512)} %param.21) | copy-start | bytes 3244
  16.8 24.1 %all-to-all-start = ((f32[32,1,1152]{2,1,0:T(1,128)}), f32[32,1,1152]{2,1,0:T(1,128)S(1)}, u32[]{:S(2)}, u32[]{:S(2)}) async-start(f32[32,1,1152]{2,1,0:T(1,128)} %copy.508), calls=%async_computation | async-start | bytes 294912 | tf_op jit(solution)/shard_map/all_to_all | solution.py:87
  53.8 5.9 %copy-start.16 = (f32[1,8,12,384]{3,1,2,0:T(8,128)S(1)}, f32[1,8,12,384]{3,1,2,0:T(8,128)}, u32[]{:S(2)}) copy-start(f32[1,8,12,384]{3,1,2,0:T(8,128)} %get-tuple-element.157) | copy-start | bytes 442372
  64.9 4.3 %copy-start.60 = (f32[288]{0:T(512)S(1)}, f32[288]{0:T(512)}, u32[]{:S(2)}) copy-start(f32[288]{0:T(512)} %reshape_squeeze.21) | copy-start | bytes 3460
  64.9 7.0 %copy-start.59 = (f32[288]{0:T(512)S(1)}, f32[288]{0:T(512)}, u32[]{:S(2)}) copy-start(f32[288]{0:T(512)} %reshape_squeeze.20) | copy-start | bytes 3460
  75.8 22.3 %all-to-all-start.1 = ((f32[32,1,1152]{2,1,0:T(1,128)}), f32[32,1,1152]{2,1,0:T(1,128)}, u32[]{:S(2)}, u32[]{:S(2)}) async-start(f32[32,1,1152]{2,1,0:T(1,128)} %copy.530), calls=%async_computation.1 | async-start | bytes 294912 | tf_op jit(solution)/shard_map/all_to_all | solution.py:140
  93.2 19.9 %collective-permute-start.1 = (f32[192,384]{1,0:T(8,128)}, f32[192,384]{1,0:T(8,128)}, u32[]{:S(2)}, u32[]{:S(2)}) collective-permute-start(f32[192,384]{1,0:T(8,128)} %pad_maximum_fusion.1), channel_id=1, source_target_pairs={{8,0},{16,8},{24,16},{32,24},{40,32},{48,40},{56,48},{64,56},{72,6... | collective-permute-start | bytes 884744 | tf_op jit(solution)/shard_map/ppermute | solution.py:13
  95.3 19.4 %collective-permute-start = (f32[192,384]{1,0:T(8,128)}, f32[192,384]{1,0:T(8,128)}, u32[]{:S(2)}, u32[]{:S(2)}) collective-permute-start(f32[192,384]{1,0:T(8,128)} %pad_maximum_fusion), channel_id=1, source_target_pairs={{248,0},{0,8},{8,16},{16,24},{24,32},{32,40},{40,48},{48,56},{56,6... | collective-permute-start | bytes 884744 | tf_op jit(solution)/shard_map/ppermute | solution.py:13
  105.6 6.1 %copy-start.42 = (f32[1,8,3,384]{3,2,1,0:T(4,128)S(1)}, f32[1,8,3,384]{3,2,1,0:T(4,128)}, u32[]{:S(2)}) copy-start(f32[1,8,3,384]{3,2,1,0:T(4,128)} %get-tuple-element.196) | copy-start | bytes 110596
  105.6 11.2 %copy-start.9 = (f32[8,1,12,384]{3,0,2,1:T(8,128)S(1)}, f32[8,1,12,384]{3,0,2,1:T(8,128)}, u32[]{:S(2)}) copy-start(f32[8,1,12,384]{3,0,2,1:T(8,128)} %get-tuple-element.124) | copy-start | bytes 442372
  146.3 24.2 %all-to-all-start.2 = ((f32[32,1,864]{2,1,0:T(1,128)}), f32[32,1,864]{2,1,0:T(1,128)}, u32[]{:S(2)}, u32[]{:S(2)}) async-start(f32[32,1,864]{2,1,0:T(1,128)} %copy.574), calls=%async_computation.2 | async-start | bytes 229376 | tf_op jit(solution)/shard_map/all_to_all | solution.py:87
  160.7 14.6 %copy-start.21 = (f32[1,8,12,384]{3,1,2,0:T(8,128)S(1)}, f32[1,8,12,384]{3,1,2,0:T(8,128)}, u32[]{:S(2)}) copy-start(f32[1,8,12,384]{3,1,2,0:T(8,128)} %get-tuple-element.115) | copy-start | bytes 442372
  160.7 14.6 %copy-start.41 = (f32[1,8,12,3]{3,1,2,0:T(8,128)S(1)}, f32[1,8,12,3]{3,1,2,0:T(8,128)}, u32[]{:S(2)}) copy-start(f32[1,8,12,3]{3,1,2,0:T(8,128)} %get-tuple-element.109) | copy-start | bytes 3460
  160.7 14.7 %copy-start.20 = (f32[1,8,12,384]{3,1,2,0:T(8,128)S(1)}, f32[1,8,12,384]{3,1,2,0:T(8,128)}, u32[]{:S(2)}) copy-start(f32[1,8,12,384]{3,1,2,0:T(8,128)} %get-tuple-element.114) | copy-start | bytes 442372
  160.7 14.7 %copy-start.40 = (f32[1,8,12,3]{3,1,2,0:T(8,128)S(1)}, f32[1,8,12,3]{3,1,2,0:T(8,128)}, u32[]{:S(2)}) copy-start(f32[1,8,12,3]{3,1,2,0:T(8,128)} %get-tuple-element.108) | copy-start | bytes 3460
  160.7 15.6 %copy-start.19 = (f32[1,8,12,384]{3,1,2,0:T(8,128)S(1)}, f32[1,8,12,384]{3,1,2,0:T(8,128)}, u32[]{:S(2)}) copy-start(f32[1,8,12,384]{3,1,2,0:T(8,128)} %get-tuple-element.113) | copy-start | bytes 442372
  160.7 15.6 %copy-start.39 = (f32[1,8,12,3]{3,1,2,0:T(8,128)S(1)}, f32[1,8,12,3]{3,1,2,0:T(8,128)}, u32[]{:S(2)}) copy-start(f32[1,8,12,3]{3,1,2,0:T(8,128)} %get-tuple-element.107) | copy-start | bytes 3460
  171.8 4.7 %copy-start.38 = (f32[1,8,12,3]{3,1,2,0:T(8,128)S(1)}, f32[1,8,12,3]{3,1,2,0:T(8,128)}, u32[]{:S(2)}) copy-start(f32[1,8,12,3]{3,1,2,0:T(8,128)} %get-tuple-element.106) | copy-start | bytes 3460
  182.0 14.6 %all-to-all-start.3 = ((f32[32,1,864]{2,1,0:T(1,128)}), f32[32,1,864]{2,1,0:T(1,128)S(1)}, u32[]{:S(2)}, u32[]{:S(2)}) async-start(f32[32,1,864]{2,1,0:T(1,128)} %copy.587), calls=%async_computation.3 | async-start | bytes 229376 | tf_op jit(solution)/shard_map/all_to_all | solution.py:140
  185.9 13.8 %collective-permute-start.2 = (f32[144,384]{1,0:T(8,128)S(1)}, f32[144,384]{1,0:T(8,128)S(1)}, u32[]{:S(2)}, u32[]{:S(2)}) collective-permute-start(f32[144,384]{1,0:T(8,128)S(1)} %reshape.3085), channel_id=1, source_target_pairs={{248,0},{0,8},{8,16},{16,24},{24,32},{32,40},{40,48},{48,56},{56,6... | collective-permute-start | bytes 663560 | tf_op jit(solution)/shard_map/ppermute | solution.py:13
  187.8 12.1 %collective-permute-start.3 = (f32[144,384]{1,0:T(8,128)S(1)}, f32[144,384]{1,0:T(8,128)S(1)}, u32[]{:S(2)}, u32[]{:S(2)}) collective-permute-start(f32[144,384]{1,0:T(8,128)S(1)} %reshape.3090), channel_id=1, source_target_pairs={{8,0},{16,8},{24,16},{32,24},{40,32},{48,40},{56,48},{64,56},{72,6... | collective-permute-start | bytes 663560 | tf_op jit(solution)/shard_map/ppermute | solution.py:13
  205.6 4.9 %copy-start.57 = (s32[270]{0:T(512)S(1)}, s32[270]{0:T(512)}, u32[]{:S(2)}) copy-start(s32[270]{0:T(512)} %copy-done.56) | copy-start | bytes 3244
  215.3 62.2 %all-to-all-start.4 = ((f32[32,136,128]{2,1,0:T(8,128)}), f32[32,136,128]{2,1,0:T(8,128)S(1)}, u32[]{:S(2)}, u32[]{:S(2)}) async-start(f32[32,136,128]{2,1,0:T(8,128)} %select_maximum_fusion), calls=%async_computation.4 | async-start | bytes 4456448 | tf_op jit(solution)/shard_map/all_to_all | solution.py:241
  278.9 19.7 %copy-start.22 = (f32[8,128,32]{1,2,0:T(8,128)}, f32[8,128,32]{1,2,0:T(8,128)S(1)}, u32[]{:S(2)}) copy-start(f32[8,128,32]{1,2,0:T(8,128)S(1)} %fusion) | copy-start | bytes 393220
  (49 other events, 78.4 us)
